TPU v7x, 512 devices: a whole 4x8x8 slice. The times are simulated.
512 devices in a mesh: dp: 8 (over z), expert: 64 (over y, x, core).
Axes of the slice: x: 4, y: 8, z: 8, core: 2. Of those that a mesh axis runs over, the one named last changes fastest.
Arguments:
- tokens: bfloat16 [65536, 1024], P(('dp', 'expert')), may hold values from -6 to 6
- expert_ids: int32 [65536, 4], P(('dp', 'expert')), may hold values from 0 to 63, all different within a row; in each aligned block of 128 rows (0 to 127, 128 to 255, ...) at most 16 rows name the same one
- gate_probs: float32 [65536, 4], P(('dp', 'expert')), may hold values from 0.05 to 1
- gate_up: bfloat16 [64, 1024, 768], P('expert', 'dp'), may hold values from -0.1875 to 0.1875
- down_proj: bfloat16 [64, 384, 1024], P('expert', None, 'dp'), may hold values from -0.3125 to 0.3125
- cotangent: bfloat16 [65536, 1024], P(('dp', 'expert')), may hold values from -0.75 to 0.75
Outputs:
- moe_out: bfloat16 [65536, 1024], P(('dp', 'expert'))
- token_grads: bfloat16 [65536, 1024], P(('dp', 'expert'))
- gate_grads: float32 [65536, 4], P(('dp', 'expert'))
- gate_up_grads: float32 [64, 1024, 768], P('expert', 'dp')
- down_grads: float32 [64, 384, 1024], P('expert', None, 'dp')
Inputs may be any that keep to these rules, and one draw needn't show every extreme that they name: `expert_ids`: each row names 4 different experts. Among the rows of one device no expert is named more than 16 times, and in every draw some device names some expert exactly 16 times.
All inputs are finite; a program needn't handle non-finite values.
Results may differ from a plain program's by a relative error of at most 0.012.
Values may be sent and summed in bfloat16 or wider, within the bound.
No kernel may reach another device: no remote copies, remote signals or barrier semaphores. Data moves between devices by JAX's collectives and lax.ppermute only.
A program may use at most 64 MiB of HBM per device.

v0:
```python
import jax
import jax.numpy as jnp
from jax import lax
from jax.sharding import PartitionSpec as P


def expert_rows(rows_in, grad_rows, weight_in, weight_out_t):
    hidden_width = weight_out_t.shape[1]
    contract_last = (((1,), (1,)), ((), ()))
    contract_first = (((0,), (0,)), ((), ()))
    pre_act = jnp.dot(rows_in, weight_in, preferred_element_type=jnp.float32)
    pre_gate = pre_act[:, :hidden_width]
    up_value = pre_act[:, hidden_width:]
    act = jax.nn.silu(pre_gate)
    hidden = (act * up_value).astype(jnp.bfloat16)
    expert_out = lax.dot_general(
        hidden, weight_out_t, contract_last, preferred_element_type=jnp.float32
    ).astype(jnp.bfloat16)
    grad_hidden = jnp.dot(grad_rows, weight_out_t, preferred_element_type=jnp.float32)
    sigmoid_value = jax.nn.sigmoid(pre_gate)
    grad_gate = grad_hidden * up_value * sigmoid_value * (1.0 + pre_gate * (1.0 - sigmoid_value))
    grad_up = grad_hidden * act
    grad_pre = jnp.concatenate([grad_gate, grad_up], axis=1).astype(jnp.bfloat16)
    grad_in = lax.dot_general(
        grad_pre, weight_in, contract_last, preferred_element_type=jnp.float32
    ).astype(jnp.bfloat16)
    weight_in_grad = lax.dot_general(
        rows_in, grad_pre, contract_first, preferred_element_type=jnp.float32
    ).astype(jnp.bfloat16)
    weight_out_grad_t = lax.dot_general(
        grad_rows, hidden, contract_first, preferred_element_type=jnp.float32
    ).astype(jnp.bfloat16)
    return (expert_out, grad_in, weight_in_grad, weight_out_grad_t)


def local(tokens, expert_ids, gate_probs, gate_up, down_proj, cotangent):
    token_count, top_count = expert_ids.shape
    width = tokens.shape[1]
    expert_count = lax.axis_size("expert")
    capacity = 2 * token_count * top_count // expert_count
    route_count = token_count * top_count
    slot_count = expert_count * capacity
    gate_width = gate_up.shape[2]
    weights = jnp.concatenate([gate_up[0], down_proj[0].T], axis=1)
    weights = lax.all_gather(weights, "dp", axis=0, tiled=True)
    weight_in = weights[:, :gate_width]
    weight_out_t = weights[:, gate_width:]
    flat_ids = expert_ids.reshape(route_count)
    onehot = (flat_ids[:, None] == jnp.arange(expert_count, dtype=jnp.int32)[None, :]).astype(
        jnp.int32
    )
    slot_index = jnp.sum((jnp.cumsum(onehot, axis=0) - onehot) * onehot, axis=1)
    position = (flat_ids * capacity + slot_index).reshape(token_count, top_count)
    slot_range = jnp.arange(slot_count, dtype=jnp.int32)
    hits = position[None, :, :] == slot_range[:, None, None]
    select = jnp.any(hits, axis=2)
    weighted = jnp.sum(jnp.where(hits, gate_probs[None, :, :], 0.0), axis=2)
    slot_probs = jnp.sum(weighted, axis=1)
    select_rows = select.astype(jnp.bfloat16)
    both = jnp.concatenate([tokens, cotangent], axis=1)
    gathered = jnp.dot(select_rows, both, preferred_element_type=jnp.float32)
    send_tokens = gathered[:, :width].astype(jnp.bfloat16)
    slot_cot = gathered[:, width:]
    send_grads = (slot_probs[:, None] * slot_cot).astype(jnp.bfloat16)
    send = jnp.concatenate([send_tokens, send_grads], axis=1)
    recv = lax.all_to_all(send, "expert", split_axis=0, concat_axis=0, tiled=True)
    rows_in = recv[:, :width]
    grad_rows = recv[:, width:]
    expert_out, grad_in, weight_in_grad, weight_out_grad_t = expert_rows(
        rows_in, grad_rows, weight_in, weight_out_t
    )
    back = lax.all_to_all(
        jnp.concatenate([expert_out, grad_in], axis=1),
        "expert",
        split_axis=0,
        concat_axis=0,
        tiled=True,
    )
    grads = lax.psum_scatter(
        jnp.concatenate([weight_in_grad, weight_out_grad_t], axis=1),
        "dp",
        scatter_dimension=0,
        tiled=True,
    ).astype(jnp.float32)
    sum_in = grads[None, :, :gate_width]
    sum_out = grads[:, gate_width:].T[None]
    back_out = back[:, :width].astype(jnp.float32)
    back_grad = back[:, width:]
    moe_out = lax.dot_general(
        weighted,
        back_out,
        (((0,), (0,)), ((), ())),
        precision=lax.Precision.HIGHEST,
        preferred_element_type=jnp.float32,
    ).astype(jnp.bfloat16)
    token_grads = lax.dot_general(
        select_rows, back_grad, (((0,), (0,)), ((), ())), preferred_element_type=jnp.float32
    ).astype(jnp.bfloat16)
    slot_gate = jnp.sum(slot_cot * back_out, axis=1)
    gate_grads = slot_gate[position]
    return (moe_out, token_grads, gate_grads, sum_in, sum_out)


def solution(mesh):
    return jax.shard_map(
        local,
        mesh=mesh,
        in_specs=(
            P(("dp", "expert"), None),
            P(("dp", "expert"), None),
            P(("dp", "expert"), None),
            P("expert", "dp", None),
            P("expert", None, "dp"),
            P(("dp", "expert"), None),
        ),
        out_specs=(
            P(("dp", "expert"), None),
            P(("dp", "expert"), None),
            P(("dp", "expert"), None),
            P("expert", "dp", None),
            P("expert", None, "dp"),
        ),
        check_vma=False,
    )
```

profile of v0, /device:TPU:2, one launch (start us, length us, event | category | flops | bytes accessed | tf_op | source)
XLA Modules:
  0.0 268.4 jit_solution(10926325315860447653)
XLA Ops:
  7.2 0.8 copy.46
  8.0 0.1 eq.42
  8.1 0.1 eq.38
  8.2 1.2 reduce-window.6
  9.4 0.2 slice_reduce_fusion
  9.7 0.1 fusion.36
  9.8 0.1 reduce_sum.39
  9.9 0.1 copy.49
  10.0 0.7 compare_select_fusion
  10.7 0.4 fusion.2
  11.0 1.0 select_reduce_fusion
  12.1 2.3 fusion.30
  14.3 0.0 copy-start
  14.3 0.3 slice.115
  14.7 2.9 %copy-done = f32[1024,2048]{1,0:T(8,128)} copy-done((f32[1024,2048]{1,0:T(8,128)}, f32[1024,2048]{1,0:T(8,128)S(1)}, u32[]{:S(2)}) %copy-start) | copy-done | bytes 8388632
  17.6 0.3 multiply_convert_fusion
  17.9 2.4 pad_maximum_fusion
  20.3 0.0 copy-start.2
  20.3 0.0 copy-start.1
  20.3 11.1 %all-to-all-start = ((bf16[64,16,2048]{2,1,0:T(8,128)(2,1)}), bf16[64,16,2048]{2,1,0:T(8,128)(2,1)}, u32[]{:S(2)}, u32[]{:S(2)}) async-start(bf16[64,16,2048]{2,1,0:T(8,128)(2,1)} %bitcast.40), calls=%async_computation | async-start | bytes 8388608 | tf_op jit(solution)/shard_map/all_to_all | solution.py:66
  31.3 0.0 all-gather.2.cloned.1.call-start
  31.4 0.0 copy-done.2
  31.4 0.1 copy.50
  31.5 0.0 copy-done.1
  31.5 0.7 pad_maximum_fusion.6
  32.3 0.0 all-gather.2.cloned.1.call-update
  32.3 51.1 %all-gather.2.cloned.1.call-done = bf16[1024,1152]{1,0:T(8,128)(2,1)} async-done(((bf16[128,1152]{1,0:T(8,128)(2,1)}), bf16[1024,1152]{1,0:T(8,128)(2,1)}) %all-gather.2.cloned.1.call-update) | async-done | bytes 2359312 | tf_op jit(solution)/shard_map/all_gather | solution.py:45
  83.4 44.2 %all-to-all-done = bf16[64,16,2048]{2,1,0:T(8,128)(2,1)} async-done(((bf16[64,16,2048]{2,1,0:T(8,128)(2,1)}), bf16[64,16,2048]{2,1,0:T(8,128)(2,1)}, u32[]{:S(2)}, u32[]{:S(2)}) %all-to-all-start) | async-done | bytes 4194336 | tf_op jit(solution)/shard_map/all_to_all | solution.py:66
  127.5 0.0 copy-start.3
  127.5 4.1 %fusion.11 = f32[1024,768]{0,1:T(8,128)S(1)} fusion(bf16[1024,2048]{1,0:T(8,128)(2,1)} %bitcast.2, bf16[1024,1152]{1,0:T(8,128)(2,1)} %all-gather.2.cloned.1.call-done), kind=kOutput, calls=%fused_computation.23 | convolution fusion | flops 1610612736 | bytes 6815744 | tf_op jit(solution)/shard_map/dot_general | solution.py:11
  131.6 0.0 copy-done.3
  131.6 3.3 %multiply_convert_fusion.2 = (bf16[1024,384]{0,1:T(8,128)(2,1)S(1)}, bf16[1024,384]{0,1:T(8,128)(2,1)S(1)}, bf16[1024,384]{0,1:T(8,128)(2,1)S(1)}) fusion(f32[1024,768]{0,1:T(8,128)S(1)} %fusion.11, bf16[1024,1152]{1,0:T(8,128)(2,1)S(1)} %copy-done.3, bf16[1024,2048]{1,0:T(8,128)(2,1)} %bitcast.2), kind=kOutput, calls=%fused_computation.28 | convolution fusion | flops 811204608 | bytes 8388608 | tf_op jit(solution)/shard_map/dot_general | solution.py:19
  134.9 1.3 convolution_convert_fusion
  136.1 1.8 convolution_convert_fusion.1
  137.9 2.4 pad_maximum_fusion.1
  140.3 6.5 %copy.51 = bf16[1024,2048]{1,0:T(8,128)(2,1)} copy(bf16[1024,2048]{0,1:T(8,128)(2,1)} %pad_maximum_fusion.1) | data formatting | bytes 8388608 | tf_op jit(solution)/shard_map/concatenate | solution.py:73
  146.8 5.9 %all-to-all-start.1 = ((bf16[64,16,2048]{2,1,0:T(8,128)(2,1)}), bf16[64,16,2048]{2,1,0:T(8,128)(2,1)}, u32[]{:S(2)}, u32[]{:S(2)}) async-start(bf16[64,16,2048]{2,1,0:T(8,128)(2,1)} %bitcast.39), calls=%async_computation.1 | async-start | bytes 8388608 | tf_op jit(solution)/shard_map/all_to_all | solution.py:72
  152.7 0.0 reduce-scatter.4.cloned.1.call-start
  152.8 2.6 fusion.17
  155.4 3.4 %fusion.13 = bf16[1024,768]{0,1:T(8,128)(2,1)S(1)} fusion(bf16[1024,2048]{1,0:T(8,128)(2,1)} %bitcast.2, bf16[1024,384]{0,1:T(8,128)(2,1)S(1)} %get-tuple-element.35, bf16[1024,384]{0,1:T(8,128)(2,1)S(1)} %get-tuple-element.34), kind=kOutput, calls=%fused_computation.25 | convolution fusion | flops 1614544896 | bytes 5242880 | tf_op jit(solution)/shard_map/dot_general | solution.py:27
  158.7 0.2 pad_maximum_fusion.2
  159.0 2.5 copy.55
  161.5 0.0 reduce-scatter.4.cloned.1.call-update
  161.5 0.1 copy.52
  161.6 0.1 reshape.45
  161.8 50.8 %reduce-scatter.4.cloned.1.call-done = bf16[128,1152]{1,0:T(8,128)(2,1)} async-done(((bf16[1024,1152]{1,0:T(8,128)(2,1)}), bf16[128,1152]{1,0:T(8,128)(2,1)}) %reduce-scatter.4.cloned.1.call-update) | async-done | bytes 294928
  212.6 1.2 copy.56
  213.8 0.9 copy.54
  214.8 0.7 slice_bitcast_fusion.1
  215.5 33.5 %all-to-all-done.1 = bf16[64,16,2048]{2,1,0:T(8,128)(2,1)} async-done(((bf16[64,16,2048]{2,1,0:T(8,128)(2,1)}), bf16[64,16,2048]{2,1,0:T(8,128)(2,1)}, u32[]{:S(2)}, u32[]{:S(2)}) %all-to-all-start.1) | async-done | bytes 4194336 | tf_op jit(solution)/shard_map/all_to_all | solution.py:72
  248.9 3.3 %multiply_reduce_fusion = f32[1024]{0:T(1024)S(1)} fusion(f32[1024,2048]{1,0:T(8,128)} %copy-done, bf16[1024,2048]{1,0:T(8,128)(2,1)} %bitcast.7), kind=kLoop, calls=%fused_computation.4 | loop fusion | flops 3144704 | bytes 6295552 | tf_op jit(solution)/shard_map/reduce_sum | solution.py:99
  252.3 2.8 %fusion.25 = bf16[128,1024]{1,0:T(8,128)(2,1)} fusion(pred[1024,128]{1,0:T(8,128)(4,1)S(1)} %fusion.2, bf16[1024,2048]{1,0:T(8,128)(2,1)} %bitcast.7), kind=kOutput, calls=%fused_computation.36 | convolution fusion | flops 268566528 | bytes 2490368 | tf_op jit(solution)/shard_map/dot_general | solution.py:96
  255.1 2.3 gather_fusion
  257.4 0.1 reshape.44
  257.5 0.7 copy.53
  258.1 3.4 %fusion.22 = bf16[128,1024]{1,0:T(8,128)(2,1)} fusion(f32[1024,128]{1,0:T(8,128)S(1)} %get-tuple-element.31, bf16[1024,2048]{1,0:T(8,128)(2,1)} %bitcast.7), kind=kOutput, calls=%fused_computation.35 | convolution fusion | flops 1610743808 | bytes 2883584 | tf_op jit(solution)/shard_map/dot_general | solution.py:89
  (6 shorter events, 0.1 us)
Async XLA Ops:
  14.3 3.2 %copy-start = (f32[1024,2048]{1,0:T(8,128)}, f32[1024,2048]{1,0:T(8,128)S(1)}, u32[]{:S(2)}) copy-start(f32[1024,2048]{1,0:T(8,128)S(1)} %fusion.30) | copy-start | bytes 25165828
  20.3 11.1 %copy-start.2 = (bf16[1,384,128]{2,1,0:T(8,128)(2,1)S(1)}, bf16[1,384,128]{2,1,0:T(8,128)(2,1)}, u32[]{:S(2)}) copy-start(bf16[1,384,128]{2,1,0:T(8,128)(2,1)} %param.10) | copy-start | bytes 294916
  20.3 11.2 %copy-start.1 = (bf16[1,128,768]{2,1,0:T(8,128)(2,1)S(1)}, bf16[1,128,768]{2,1,0:T(8,128)(2,1)}, u32[]{:S(2)}) copy-start(bf16[1,128,768]{2,1,0:T(8,128)(2,1)} %param.9) | copy-start | bytes 589828
  20.3 107.3 %all-to-all-start = ((bf16[64,16,2048]{2,1,0:T(8,128)(2,1)}), bf16[64,16,2048]{2,1,0:T(8,128)(2,1)}, u32[]{:S(2)}, u32[]{:S(2)}) async-start(bf16[64,16,2048]{2,1,0:T(8,128)(2,1)} %bitcast.40), calls=%async_computation | async-start | bytes 8388608 | tf_op jit(solution)/shard_map/all_to_all | solution.py:66
  31.3 52.0 %all-gather.2.cloned.1.call-start = ((), (), s32[]{:S(2)}) async-start(), calls=%async_computation.3 | async-start | bytes 2654208 | tf_op jit(solution)/shard_map/all_gather | solution.py:45
  127.5 4.1 %copy-start.3 = (bf16[1024,1152]{1,0:T(8,128)(2,1)S(1)}, bf16[1024,1152]{1,0:T(8,128)(2,1)}, u32[]{:S(2)}) copy-start(bf16[1024,1152]{1,0:T(8,128)(2,1)} %all-gather.2.cloned.1.call-done) | copy-start | bytes 7077892
  146.8 102.1 %all-to-all-start.1 = ((bf16[64,16,2048]{2,1,0:T(8,128)(2,1)}), bf16[64,16,2048]{2,1,0:T(8,128)(2,1)}, u32[]{:S(2)}, u32[]{:S(2)}) async-start(bf16[64,16,2048]{2,1,0:T(8,128)(2,1)} %bitcast.39), calls=%async_computation.1 | async-start | bytes 8388608 | tf_op jit(solution)/shard_map/all_to_all | solution.py:72
  152.7 59.9 %reduce-scatter.4.cloned.1.call-start = ((), (), s32[]{:S(2)}) async-start(), calls=%async_computation.4 | async-start | bytes 2654208
Sparse Core Ops, SparseCore 0:
  34.8 48.5 all-gather.1
  161.6 50.9 reduce-scatter.3
where the time goes:
time: 269 us; the launch traced here: 268 us
  waiting for transfers between devices  180 us (67%)
  matrix products  24.8 us (9%)
  local copies, waits for them, and re-layouts  19.8 us (7%)
  starting transfers between devices  17 us (6%)
  between operations  14.2 us (5%)
  other arithmetic  12.9 us (5%)
    all_gather x1, waiting for transfers between devices, local(): weights = lax.all_gather(weights, 'dp', axis=0, tiled=True)  51.1 us
    unnamed x3, waiting for transfers between devices  50.9 us
    all_to_all x1, waiting for transfers between devices, local(): lax.all_to_all(send, 'expert', split_axis=0, concat_axis=0, tiled=True)  44.2 us
    all_to_all x1, waiting for transfers between devices, local(): lax.all_to_all(jnp.concatenate([expert_out, grad_in], axis=1), 'expert',...  33.5 us
    all_to_all x1, starting transfers between devices, local(): lax.all_to_all(send, 'expert', split_axis=0, concat_axis=0, tiled=True)  11.1 us
    unnamed x13, local copies, waits for them, and re-layouts  8.95 us
    concatenate x1, local copies, waits for them, and re-layouts, local(): jnp.concatenate([expert_out, grad_in], axis=1)  6.49 us
    all_to_all x1, starting transfers between devices, local(): lax.all_to_all(jnp.concatenate([expert_out, grad_in], axis=1), 'expert',...  5.88 us
  transfers between devices with their start and end apart: 4, of which 4 were waited for; matrix products, arithmetic and copies ran while one was open for 5% of the time, Pallas kernels for 0%

commit v1 on v0

--- a/solution.py
+++ b/solution.py
@@ -2,6 +2,27 @@
 import jax.numpy as jnp
 from jax import lax
 from jax.sharding import PartitionSpec as P
+
+
+def ring_gather(value, axis, dim):
+    count, here, width = (lax.axis_size(axis), lax.axis_index(axis), value.shape[dim])
+    ahead = [(i, (i + 1) % count) for i in range(count)]
+    backward = [(i, (i - 1) % count) for i in range(count)]
+    whole = jnp.zeros((*value.shape[:dim], count * width, *value.shape[dim + 1 :]), value.dtype)
+    whole = lax.dynamic_update_slice_in_dim(whole, value, here * width, axis=dim)
+    from_left = from_right = value
+    half = count // 2
+    for step in range(1, half + 1):
+        from_left = lax.ppermute(from_left, axis, ahead)
+        whole = lax.dynamic_update_slice_in_dim(
+            whole, from_left, (here - step) % count * width, axis=dim
+        )
+        if step < count - half:
+            from_right = lax.ppermute(from_right, axis, backward)
+            whole = lax.dynamic_update_slice_in_dim(
+                whole, from_right, (here + step) % count * width, axis=dim
+            )
+    return whole
 
 
 def expert_rows(rows_in, grad_rows, weight_in, weight_out_t):
@@ -42,7 +63,7 @@
     slot_count = expert_count * capacity
     gate_width = gate_up.shape[2]
     weights = jnp.concatenate([gate_up[0], down_proj[0].T], axis=1)
-    weights = lax.all_gather(weights, "dp", axis=0, tiled=True)
+    weights = ring_gather(weights, "dp", 0)
     weight_in = weights[:, :gate_width]
     weight_out_t = weights[:, gate_width:]
     flat_ids = expert_ids.reshape(route_count)

time: 269 us -> 269 us (level)
  waiting for transfers between devices: 180 us -> 147 us
  starting transfers between devices: 17 us -> 46.1 us
    all_gather x1 -> x0, waiting for transfers between devices: 51.1 us -> none  [local(): weights = lax.all_gather(weights, 'dp', axis=0, tiled=True)]
    ppermute x0 -> x7, starting transfers between devices: none -> 29 us  [the longest x3 18.9 us: ring_gather(): from_right = lax.ppermute(from_right, axis, backward)]
    ppermute x0 -> x7, waiting for transfers between devices: none -> 19.5 us  [the longest x4 19.5 us: ring_gather(): from_left = lax.ppermute(from_left, axis, ahead)]
    unnamed x13 -> x21, local copies, waits for them, and re-layouts: 8.95 us -> 9.07 us
    unnamed x3 -> x2, waiting for transfers between devices: 50.9 us -> 50.8 us
  transfers between devices with their start and end apart: 4 -> 10, of which waited for: 4 -> 7; matrix products, arithmetic and copies ran while one was open for 5% -> 6% of each run, Pallas kernels for 0% -> 0%
where the time goes in v1:
time: 269 us; the launch traced here: 268 us
  waiting for transfers between devices  147 us (55%)
  starting transfers between devices  46.1 us (17%)
  matrix products  24.3 us (9%)
  local copies, waits for them, and re-layouts  22.3 us (8%)
  between operations  14.5 us (5%)
  other arithmetic  13.1 us (5%)
    unnamed x2, waiting for transfers between devices  50.8 us
    all_to_all x1, waiting for transfers between devices, local(): lax.all_to_all(send, 'expert', split_axis=0, concat_axis=0, tiled=True)  44 us
    all_to_all x1, waiting for transfers between devices, local(): lax.all_to_all(jnp.concatenate([expert_out, grad_in], axis=1), 'expert',...  33.1 us
    ppermute x4, waiting for transfers between devices, ring_gather(): from_left = lax.ppermute(from_left, axis, ahead)  19.5 us
    ppermute x3, starting transfers between devices, ring_gather(): from_right = lax.ppermute(from_right, axis, backward)  18.9 us
    all_to_all x1, starting transfers between devices, local(): lax.all_to_all(send, 'expert', split_axis=0, concat_axis=0, tiled=True)  11 us
    ppermute x4, starting transfers between devices, ring_gather(): from_left = lax.ppermute(from_left, axis, ahead)  10.1 us
    unnamed x21, local copies, waits for them, and re-layouts  9.07 us
  transfers between devices with their start and end apart: 10, of which 7 were waited for; matrix products, arithmetic and copies ran while one was open for 6% of the time, Pallas kernels for 0%

profile of v1, /device:TPU:2, one launch (start us, length us, event | category | flops | bytes accessed | tf_op | source)
XLA Modules:
  0.0 267.8 jit_solution(472551911405040846)
XLA Ops:
  7.2 0.8 copy.46
  8.0 0.1 eq.50
  8.1 0.1 eq.46
  8.2 1.2 reduce-window.6
  9.4 0.2 slice_reduce_fusion
  9.7 0.1 fusion.36
  9.8 0.1 reduce_sum.39
  9.9 0.1 copy.49
  10.0 0.7 compare_select_fusion
  10.7 0.4 fusion.2
  11.0 1.0 select_reduce_fusion
  12.1 2.3 fusion.30
  14.3 0.3 slice.115
  14.7 2.9 %copy-done = f32[1024,2048]{1,0:T(8,128)} copy-done((f32[1024,2048]{1,0:T(8,128)}, f32[1024,2048]{1,0:T(8,128)S(1)}, u32[]{:S(2)}) %copy-start) | copy-done | bytes 8388632
  17.6 0.3 multiply_convert_fusion
  17.9 2.4 pad_maximum_fusion
  20.3 11.0 %all-to-all-start = ((bf16[64,16,2048]{2,1,0:T(8,128)(2,1)}), bf16[64,16,2048]{2,1,0:T(8,128)(2,1)}, u32[]{:S(2)}, u32[]{:S(2)}) async-start(bf16[64,16,2048]{2,1,0:T(8,128)(2,1)} %bitcast.39), calls=%async_computation | async-start | bytes 8388608 | tf_op jit(solution)/shard_map/all_to_all | solution.py:87
  31.3 0.1 copy.50
  31.5 0.2 broadcast_in_dim.30
  31.6 1.0 pad_maximum_fusion.6
  32.6 4.2 %collective-permute-start = (bf16[128,1152]{1,0:T(8,128)(2,1)S(1)}, bf16[128,1152]{1,0:T(8,128)(2,1)}, u32[]{:S(2)}, u32[]{:S(2)}) collective-permute-start(bf16[128,1152]{1,0:T(8,128)(2,1)S(1)} %get-tuple-element.37), channel_id=1, source_target_pairs={{0,64},{64,128},{128,192},{192,256},{256,320},{320,384},{384,448},... | collective-permute-start | bytes 884744 | tf_op jit(solution)/shard_map/ppermute | solution.py:16
  36.8 8.6 %collective-permute-start.1 = (bf16[128,1152]{1,0:T(8,128)(2,1)S(1)}, bf16[128,1152]{1,0:T(8,128)(2,1)}, u32[]{:S(2)}, u32[]{:S(2)}) collective-permute-start(bf16[128,1152]{1,0:T(8,128)(2,1)S(1)} %get-tuple-element.37), channel_id=1, source_target_pairs={{0,448},{64,0},{128,64},{192,128},{256,192},{320,256},{384,320},{4... | collective-permute-start | bytes 884744 | tf_op jit(solution)/shard_map/ppermute | solution.py:21
  45.6 5.3 %collective-permute-done = bf16[128,1152]{1,0:T(8,128)(2,1)} collective-permute-done((bf16[128,1152]{1,0:T(8,128)(2,1)S(1)}, bf16[128,1152]{1,0:T(8,128)(2,1)}, u32[]{:S(2)}, u32[]{:S(2)}) %collective-permute-start) | collective-permute-done | bytes 294944 | tf_op jit(solution)/shard_map/ppermute | solution.py:16
  50.9 1.9 collective-permute-start.2
  52.8 0.0 collective-permute-done.1
  52.8 5.1 %collective-permute-start.3 = (bf16[128,1152]{1,0:T(8,128)(2,1)}, bf16[128,1152]{1,0:T(8,128)(2,1)S(1)}, u32[]{:S(2)}, u32[]{:S(2)}) collective-permute-start(bf16[128,1152]{1,0:T(8,128)(2,1)} %collective-permute-done.1), channel_id=1, source_target_pairs={{0,448},{64,0},{128,64},{192,128},{256,192},{320,256},{384,320},{4... | collective-permute-start | bytes 884744 | tf_op jit(solution)/shard_map/ppermute | solution.py:21
  57.9 1.0 constant_dynamic-update-slice_fusion.6
  58.9 1.0 constant_dynamic-update-slice_fusion.5
  59.9 2.7 %collective-permute-done.2 = bf16[128,1152]{1,0:T(8,128)(2,1)S(1)} collective-permute-done((bf16[128,1152]{1,0:T(8,128)(2,1)}, bf16[128,1152]{1,0:T(8,128)(2,1)S(1)}, u32[]{:S(2)}, u32[]{:S(2)}) %collective-permute-start.2) | collective-permute-done | bytes 294944 | tf_op jit(solution)/shard_map/ppermute | solution.py:16
  62.6 1.9 collective-permute-start.4
  64.6 0.0 collective-permute-done.3
  64.6 5.1 %collective-permute-start.5 = (bf16[128,1152]{1,0:T(8,128)(2,1)S(1)}, bf16[128,1152]{1,0:T(8,128)(2,1)S(1)}, u32[]{:S(2)}, u32[]{:S(2)}) collective-permute-start(bf16[128,1152]{1,0:T(8,128)(2,1)S(1)} %collective-permute-done.3), channel_id=1, source_target_pairs={{0,448},{64,0},{128,64},{192,128},{256,192},{320,256},{384,320},{4... | collective-permute-start | bytes 884744 | tf_op jit(solution)/shard_map/ppermute | solution.py:21
  69.8 3.6 %collective-permute-done.4 = bf16[128,1152]{1,0:T(8,128)(2,1)S(1)} collective-permute-done((bf16[128,1152]{1,0:T(8,128)(2,1)S(1)}, bf16[128,1152]{1,0:T(8,128)(2,1)S(1)}, u32[]{:S(2)}, u32[]{:S(2)}) %collective-permute-start.4) | collective-permute-done | bytes 294944 | tf_op jit(solution)/shard_map/ppermute | solution.py:16
  73.4 2.1 collective-permute-start.6
  75.6 0.0 collective-permute-done.5
  75.6 7.8 %collective-permute-done.6 = bf16[128,1152]{1,0:T(8,128)(2,1)S(1)} collective-permute-done((bf16[128,1152]{1,0:T(8,128)(2,1)S(1)}, bf16[128,1152]{1,0:T(8,128)(2,1)S(1)}, u32[]{:S(2)}, u32[]{:S(2)}) %collective-permute-start.6) | collective-permute-done | bytes 294944 | tf_op jit(solution)/shard_map/ppermute | solution.py:16
  83.5 44.0 %all-to-all-done = bf16[64,16,2048]{2,1,0:T(8,128)(2,1)} async-done(((bf16[64,16,2048]{2,1,0:T(8,128)(2,1)}), bf16[64,16,2048]{2,1,0:T(8,128)(2,1)}, u32[]{:S(2)}, u32[]{:S(2)}) %all-to-all-start) | async-done | bytes 4194336 | tf_op jit(solution)/shard_map/all_to_all | solution.py:87
  127.5 3.5 %fusion.11 = f32[1024,768]{0,1:T(8,128)S(1)} fusion(bf16[1024,2048]{1,0:T(8,128)(2,1)} %bitcast.2, bf16[1024,1152]{1,0:T(8,128)(2,1)S(1)} %constant_dynamic-update-slice_fusion), kind=kOutput, calls=%fused_computation.23 | convolution fusion | flops 1610612736 | bytes 6815744 | tf_op jit(solution)/shard_map/dot_general | solution.py:32
  131.0 3.3 %multiply_convert_fusion.2 = (bf16[1024,384]{0,1:T(8,128)(2,1)S(1)}, bf16[1024,384]{0,1:T(8,128)(2,1)S(1)}, bf16[1024,384]{0,1:T(8,128)(2,1)S(1)}) fusion(f32[1024,768]{0,1:T(8,128)S(1)} %fusion.11, bf16[1024,1152]{1,0:T(8,128)(2,1)S(1)} %constant_dynamic-update-slice_fusion, bf16[1024,2048]{1,0:T(8,128)(2,1)} %bitcast.2), kind=kOutput, calls=%fused_computation.28 | convolution fusion | flops 811204608 | bytes 8388608 | tf_op jit(solution)/shard_map/dot_general | solution.py:40
  134.3 1.3 convolution_convert_fusion
  135.6 0.1 copy-done.6
  135.7 1.8 convolution_convert_fusion.1
  137.5 2.4 pad_maximum_fusion.1
  139.9 6.5 %copy.51 = bf16[1024,2048]{1,0:T(8,128)(2,1)} copy(bf16[1024,2048]{0,1:T(8,128)(2,1)} %pad_maximum_fusion.1) | data formatting | bytes 8388608 | tf_op jit(solution)/shard_map/concatenate | solution.py:94
  146.4 5.8 %all-to-all-start.1 = ((bf16[64,16,2048]{2,1,0:T(8,128)(2,1)}), bf16[64,16,2048]{2,1,0:T(8,128)(2,1)}, u32[]{:S(2)}, u32[]{:S(2)}) async-start(bf16[64,16,2048]{2,1,0:T(8,128)(2,1)} %bitcast.40), calls=%async_computation.1 | async-start | bytes 8388608 | tf_op jit(solution)/shard_map/all_to_all | solution.py:93
  152.2 0.3 reduce-scatter.4.cloned.1.call-start
  152.5 2.7 %fusion.17 = bf16[1024,384]{0,1:T(8,128)(2,1)S(1)} fusion(bf16[1024,384]{0,1:T(8,128)(2,1)S(1)} %copy-done.3, bf16[1024,2048]{1,0:T(8,128)(2,1)} %bitcast.2), kind=kOutput, calls=%fused_computation.32 | convolution fusion | flops 805699584 | bytes 3670016 | tf_op jit(solution)/shard_map/dot_general | solution.py:51
  155.2 3.4 %fusion.13 = bf16[1024,768]{0,1:T(8,128)(2,1)S(1)} fusion(bf16[1024,2048]{1,0:T(8,128)(2,1)} %bitcast.2, bf16[1024,384]{0,1:T(8,128)(2,1)S(1)} %copy-done.7, bf16[1024,384]{0,1:T(8,128)(2,1)S(1)} %copy-done.5), kind=kOutput, calls=%fused_computation.25 | convolution fusion | flops 1614544896 | bytes 5242880 | tf_op jit(solution)/shard_map/dot_general | solution.py:48
  158.6 0.2 pad_maximum_fusion.2
  158.9 2.5 copy.55
  161.4 0.0 reduce-scatter.4.cloned.1.call-update
  161.4 0.1 copy.52
  161.5 0.1 reshape.45
  161.6 50.8 %reduce-scatter.4.cloned.1.call-done = bf16[128,1152]{1,0:T(8,128)(2,1)} async-done(((bf16[1024,1152]{1,0:T(8,128)(2,1)}), bf16[128,1152]{1,0:T(8,128)(2,1)}) %reduce-scatter.4.cloned.1.call-update) | async-done | bytes 294928
  212.4 1.2 copy.56
  213.7 0.9 copy.54
  214.6 0.7 slice_bitcast_fusion.1
  215.3 33.1 %all-to-all-done.1 = bf16[64,16,2048]{2,1,0:T(8,128)(2,1)} async-done(((bf16[64,16,2048]{2,1,0:T(8,128)(2,1)}), bf16[64,16,2048]{2,1,0:T(8,128)(2,1)}, u32[]{:S(2)}, u32[]{:S(2)}) %all-to-all-start.1) | async-done | bytes 4194336 | tf_op jit(solution)/shard_map/all_to_all | solution.py:93
  248.4 3.3 %multiply_reduce_fusion = f32[1024]{0:T(1024)S(1)} fusion(f32[1024,2048]{1,0:T(8,128)} %copy-done, bf16[1024,2048]{1,0:T(8,128)(2,1)} %bitcast.7), kind=kLoop, calls=%fused_computation.4 | loop fusion | flops 3144704 | bytes 6295552 | tf_op jit(solution)/shard_map/reduce_sum | solution.py:120
  251.7 2.8 %fusion.25 = bf16[128,1024]{1,0:T(8,128)(2,1)} fusion(pred[1024,128]{1,0:T(8,128)(4,1)S(1)} %fusion.2, bf16[1024,2048]{1,0:T(8,128)(2,1)} %bitcast.7), kind=kOutput, calls=%fused_computation.36 | convolution fusion | flops 268566528 | bytes 2490368 | tf_op jit(solution)/shard_map/dot_general | solution.py:117
  254.5 2.3 gather_fusion
  256.8 0.1 reshape.44
  256.9 0.7 copy.53
  257.6 3.4 %fusion.22 = bf16[128,1024]{1,0:T(8,128)(2,1)} fusion(f32[1024,128]{1,0:T(8,128)S(1)} %get-tuple-element.31, bf16[1024,2048]{1,0:T(8,128)(2,1)} %bitcast.7), kind=kOutput, calls=%fused_computation.35 | convolution fusion | flops 1610743808 | bytes 2883584 | tf_op jit(solution)/shard_map/dot_general | solution.py:110
  (25 shorter events, 0.3 us)
Async XLA Ops:
  14.3 3.2 %copy-start = (f32[1024,2048]{1,0:T(8,128)}, f32[1024,2048]{1,0:T(8,128)S(1)}, u32[]{:S(2)}) copy-start(f32[1024,2048]{1,0:T(8,128)S(1)} %fusion.30) | copy-start | bytes 25165828
  20.3 11.1 %copy-start.1 = (bf16[1,384,128]{2,1,0:T(8,128)(2,1)S(1)}, bf16[1,384,128]{2,1,0:T(8,128)(2,1)}, u32[]{:S(2)}) copy-start(bf16[1,384,128]{2,1,0:T(8,128)(2,1)} %param.10) | copy-start | bytes 294916
  20.3 107.3 %all-to-all-start = ((bf16[64,16,2048]{2,1,0:T(8,128)(2,1)}), bf16[64,16,2048]{2,1,0:T(8,128)(2,1)}, u32[]{:S(2)}, u32[]{:S(2)}) async-start(bf16[64,16,2048]{2,1,0:T(8,128)(2,1)} %bitcast.39), calls=%async_computation | async-start | bytes 8388608 | tf_op jit(solution)/shard_map/all_to_all | solution.py:87
  32.6 18.3 %collective-permute-start = (bf16[128,1152]{1,0:T(8,128)(2,1)S(1)}, bf16[128,1152]{1,0:T(8,128)(2,1)}, u32[]{:S(2)}, u32[]{:S(2)}) collective-permute-start(bf16[128,1152]{1,0:T(8,128)(2,1)S(1)} %get-tuple-element.37), channel_id=1, source_target_pairs={{0,64},{64,128},{128,192},{192,256},{256,320},{320,384},{384,448},... | collective-permute-start | bytes 884744 | tf_op jit(solution)/shard_map/ppermute | solution.py:16
  36.8 16.0 %collective-permute-start.1 = (bf16[128,1152]{1,0:T(8,128)(2,1)S(1)}, bf16[128,1152]{1,0:T(8,128)(2,1)}, u32[]{:S(2)}, u32[]{:S(2)}) collective-permute-start(bf16[128,1152]{1,0:T(8,128)(2,1)S(1)} %get-tuple-element.37), channel_id=1, source_target_pairs={{0,448},{64,0},{128,64},{192,128},{256,192},{320,256},{384,320},{4... | collective-permute-start | bytes 884744 | tf_op jit(solution)/shard_map/ppermute | solution.py:21
  50.9 11.8 %collective-permute-start.2 = (bf16[128,1152]{1,0:T(8,128)(2,1)}, bf16[128,1152]{1,0:T(8,128)(2,1)S(1)}, u32[]{:S(2)}, u32[]{:S(2)}) collective-permute-start(bf16[128,1152]{1,0:T(8,128)(2,1)} %collective-permute-done), channel_id=1, source_target_pairs={{0,64},{64,128},{128,192},{192,256},{256,320},{320,384},{384,448},... | collective-permute-start | bytes 884744 | tf_op jit(solution)/shard_map/ppermute | solution.py:16
  52.8 11.7 %collective-permute-start.3 = (bf16[128,1152]{1,0:T(8,128)(2,1)}, bf16[128,1152]{1,0:T(8,128)(2,1)S(1)}, u32[]{:S(2)}, u32[]{:S(2)}) collective-permute-start(bf16[128,1152]{1,0:T(8,128)(2,1)} %collective-permute-done.1), channel_id=1, source_target_pairs={{0,448},{64,0},{128,64},{192,128},{256,192},{320,256},{384,320},{4... | collective-permute-start | bytes 884744 | tf_op jit(solution)/shard_map/ppermute | solution.py:21
  62.6 10.8 %collective-permute-start.4 = (bf16[128,1152]{1,0:T(8,128)(2,1)S(1)}, bf16[128,1152]{1,0:T(8,128)(2,1)S(1)}, u32[]{:S(2)}, u32[]{:S(2)}) collective-permute-start(bf16[128,1152]{1,0:T(8,128)(2,1)S(1)} %collective-permute-done.2), channel_id=1, source_target_pairs={{0,64},{64,128},{128,192},{192,256},{256,320},{320,384},{384,448},... | collective-permute-start | bytes 884744 | tf_op jit(solution)/shard_map/ppermute | solution.py:16
  64.6 11.0 %collective-permute-start.5 = (bf16[128,1152]{1,0:T(8,128)(2,1)S(1)}, bf16[128,1152]{1,0:T(8,128)(2,1)S(1)}, u32[]{:S(2)}, u32[]{:S(2)}) collective-permute-start(bf16[128,1152]{1,0:T(8,128)(2,1)S(1)} %collective-permute-done.3), channel_id=1, source_target_pairs={{0,448},{64,0},{128,64},{192,128},{256,192},{320,256},{384,320},{4... | collective-permute-start | bytes 884744 | tf_op jit(solution)/shard_map/ppermute | solution.py:21
  73.4 10.0 %collective-permute-start.6 = (bf16[128,1152]{1,0:T(8,128)(2,1)S(1)}, bf16[128,1152]{1,0:T(8,128)(2,1)S(1)}, u32[]{:S(2)}, u32[]{:S(2)}) collective-permute-start(bf16[128,1152]{1,0:T(8,128)(2,1)S(1)} %collective-permute-done.4), channel_id=1, source_target_pairs={{0,64},{64,128},{128,192},{192,256},{256,320},{320,384},{384,448},... | collective-permute-start | bytes 884744 | tf_op jit(solution)/shard_map/ppermute | solution.py:16
  134.2 1.3 copy-start.2
  134.3 1.3 copy-start.4
  134.3 1.4 copy-start.6
  146.4 6.1 %copy-start.3 = (bf16[1024,384]{0,1:T(8,128)(2,1)S(1)}, bf16[1024,384]{0,1:T(8,128)(2,1)}, u32[]{:S(2)}) copy-start(bf16[1024,384]{0,1:T(8,128)(2,1)} %copy-done.2) | copy-start | bytes 2359300
  146.4 102.0 %all-to-all-start.1 = ((bf16[64,16,2048]{2,1,0:T(8,128)(2,1)}), bf16[64,16,2048]{2,1,0:T(8,128)(2,1)}, u32[]{:S(2)}, u32[]{:S(2)}) async-start(bf16[64,16,2048]{2,1,0:T(8,128)(2,1)} %bitcast.40), calls=%async_computation.1 | async-start | bytes 8388608 | tf_op jit(solution)/shard_map/all_to_all | solution.py:93
  152.2 3.0 %copy-start.5 = (bf16[1024,384]{0,1:T(8,128)(2,1)S(1)}, bf16[1024,384]{0,1:T(8,128)(2,1)}, u32[]{:S(2)}) copy-start(bf16[1024,384]{0,1:T(8,128)(2,1)} %copy-done.4) | copy-start | bytes 2359300
  152.2 3.0 %copy-start.7 = (bf16[1024,384]{0,1:T(8,128)(2,1)S(1)}, bf16[1024,384]{0,1:T(8,128)(2,1)}, u32[]{:S(2)}) copy-start(bf16[1024,384]{0,1:T(8,128)(2,1)} %copy-done.6) | copy-start | bytes 2359300
  152.2 60.2 %reduce-scatter.4.cloned.1.call-start = ((), (), s32[]{:S(2)}) async-start(), calls=%async_computation.3 | async-start | bytes 2654208
Sparse Core Ops, SparseCore 0:
  161.5 50.8 reduce-scatter.3
